TPU v7x, 256 devices: a whole 4x4x8 slice. The times are simulated.
256 devices in a mesh: expert: 32 (over z_lo, x, core), replica: 8 (over z_hi, y).
Axes of the slice: x: 4, y: 4, z: 8 (z_hi: 2, z_lo: 4; z = z_hi * 4 + z_lo), core: 2. Of those that a mesh axis runs over, the one named last changes fastest.
Arguments:
- tokens: bfloat16 [2048, 4096], P(('expert', 'replica')), may hold values from -6 to 6
- expert_ids: int32 [2048, 8], P(('expert', 'replica')), may hold values from 0 to 31, as said below
- gate_weights: float32 [2048, 8], P(('expert', 'replica')), may hold values from 0.1 to 1
- expert_holder: int32 [32], replicated, may hold values from 0 to 31, each once
- swap_pairs: int32 [8, 2], replicated, may hold values from 0 to 31, as said below
- capacity: int32 [32], replicated, may hold values from 2 to 4, as said below
- w_gate: bfloat16 [32, 1536, 4096], P('expert', 'replica'), may hold values from -0.09375 to 0.09375
- w_up: bfloat16 [32, 1536, 4096], P('expert', 'replica'), may hold values from -0.09375 to 0.09375
- w_down: bfloat16 [32, 1536, 4096], P('expert', 'replica'), may hold values from -0.15625 to 0.15625
Outputs:
- moe_output: bfloat16 [2048, 4096], P(('expert', 'replica'))
- moved_gate: bfloat16 [32, 1536, 4096], P('expert', 'replica')
- moved_up: bfloat16 [32, 1536, 4096], P('expert', 'replica')
- moved_down: bfloat16 [32, 1536, 4096], P('expert', 'replica')
- expert_peak: float32 [32], P('expert')
Inputs may be any that keep to these rules, and one draw needn't show every extreme that they name: `expert_ids`: each token names 8 different experts; among one device's 8 tokens no expert is named more than 4 times, and one expert is named exactly 4 times by the tokens of every device. `swap_pairs`: no index appears twice; the two indices of every pair differ by 16. The expert named 4 times by every device has capacity 4. `expert_holder`: each index of the expert axis holds one expert.
All inputs are finite; a program needn't handle non-finite values.
Results may differ from a plain program's by a relative error of at most 0.014.
Values may be sent and summed in bfloat16 or wider, within the bound.
No kernel may reach another device: no remote copies, remote signals or barrier semaphores. Data moves between devices by JAX's collectives and lax.ppermute only.
A program may use at most 128 MiB of HBM per device.

v0:
```python
import jax
import jax.numpy as jnp
from jax import lax
from jax.sharding import PartitionSpec as P

TOPK = 8
CAP = 4


def pair_partner(swap_pairs, device_count):
    devices = jnp.arange(device_count, dtype=jnp.int32)
    first_dev = swap_pairs[:, 0:1]
    second_dev = swap_pairs[:, 1:2]
    offsets = jnp.where(devices[None, :] == first_dev, second_dev - first_dev, 0)
    offsets = offsets + jnp.where(devices[None, :] == second_dev, first_dev - second_dev, 0)
    return devices + jnp.sum(offsets, axis=0)


def table_lookup(values_table, positions):
    matches = positions[..., None] == jnp.arange(values_table.shape[0], dtype=jnp.int32)
    return jnp.sum(jnp.where(matches, values_table, 0), axis=-1)


def route_slots(expert_ids, holder_now, capacity):
    expert_count = holder_now.shape[0]
    flat_ids = expert_ids.reshape(-1)
    chosen = (flat_ids[:, None] == jnp.arange(expert_count, dtype=jnp.int32)[None, :]).astype(
        jnp.int32
    )
    earlier = jnp.cumsum(chosen, axis=0) - chosen
    ranking = jnp.sum(earlier * chosen, axis=1)
    slot_kept = ranking < table_lookup(capacity, flat_ids)
    target = table_lookup(holder_now, flat_ids)
    slot_ids = jnp.where(slot_kept, target * CAP + ranking, -1)
    matched = slot_ids[None, :] == jnp.arange(expert_count * CAP, dtype=jnp.int32)[:, None]
    owners = jnp.arange(flat_ids.shape[0], dtype=jnp.int32) // TOPK
    source = jnp.sum(jnp.where(matched, owners[None, :], 0), axis=1)
    filled = jnp.any(matched, axis=1)
    return (jnp.maximum(slot_ids, 0), slot_kept, source, filled)


def expert_hidden(row_block, gate_local, up_local):
    leading = row_block.shape[:-1]
    row_matrix = row_block.reshape(-1, row_block.shape[-1])
    contract = (((1,), (1,)), ((), ()))
    gate_value = lax.dot_general(
        row_matrix, gate_local, contract, preferred_element_type=jnp.float32
    )
    up_value = lax.dot_general(row_matrix, up_local, contract, preferred_element_type=jnp.float32)
    hidden = (jax.nn.silu(gate_value) * up_value).astype(jnp.bfloat16)
    return hidden.reshape(leading + (gate_local.shape[0],))


def shards(
    tokens, expert_ids, gate_weights, expert_holder, swap_pairs, capacity, w_gate, w_up, w_down
):
    experts = lax.axis_size("expert")
    replicas = lax.axis_size("replica")
    tok_rows, width = tokens.shape
    partner = pair_partner(swap_pairs, experts)
    holder_after = table_lookup(partner, expert_holder)
    spread = (
        lax.all_to_all(
            w_gate.reshape(experts, -1), "expert", split_axis=0, concat_axis=0, tiled=True
        ),
        lax.all_to_all(
            w_up.reshape(experts, -1), "expert", split_axis=0, concat_axis=0, tiled=True
        ),
        lax.all_to_all(
            w_down.reshape(experts, -1), "expert", split_axis=0, concat_axis=0, tiled=True
        ),
    )
    arranged = tuple((jnp.take(pieces, partner, axis=0) for pieces in spread))
    moved = (
        lax.all_to_all(arranged[0], "expert", split_axis=0, concat_axis=0, tiled=True),
        lax.all_to_all(arranged[1], "expert", split_axis=0, concat_axis=0, tiled=True),
        lax.all_to_all(arranged[2], "expert", split_axis=0, concat_axis=0, tiled=True),
    )
    moved_gate = moved[0].reshape(w_gate.shape)
    moved_up = moved[1].reshape(w_up.shape)
    moved_down = moved[2].reshape(w_down.shape)
    gate_local, up_local, down_local = (moved_gate[0], moved_up[0], moved_down[0])
    group_tokens, group_ids = (
        lax.all_gather(tokens, "replica", axis=0, tiled=True),
        lax.all_gather(expert_ids, "replica", axis=0, tiled=True),
    )
    group_ids = group_ids.reshape(replicas, tok_rows, TOPK)
    slot_all, kept_all, source_all, filled_all = jax.vmap(route_slots, in_axes=(0, None, None))(
        group_ids, holder_after, capacity
    )
    starts = jnp.arange(replicas, dtype=jnp.int32)[:, None] * tok_rows
    picked = jnp.take(group_tokens, source_all + starts, axis=0)
    outgoing = jnp.where(filled_all[:, :, None], picked, jnp.zeros((), jnp.bfloat16))
    hidden = expert_hidden(
        lax.all_to_all(
            outgoing.reshape(replicas, experts, CAP, width),
            "expert",
            split_axis=1,
            concat_axis=1,
            tiled=True,
        ),
        gate_local,
        up_local,
    )
    replica_index = lax.axis_index("replica")
    slot_of = lax.dynamic_index_in_dim(slot_all, replica_index, 0, keepdims=False)
    slot_kept = lax.dynamic_index_in_dim(kept_all, replica_index, 0, keepdims=False)
    hidden_rows = hidden.reshape(-1, hidden.shape[-1])
    local_peak = jnp.max(jnp.abs(hidden_rows)).astype(jnp.float32)
    summed = lax.psum_scatter(
        jnp.dot(hidden_rows, down_local, preferred_element_type=jnp.float32).astype(jnp.bfloat16),
        "replica",
        scatter_dimension=0,
        tiled=True,
    )
    results = summed.reshape(experts, CAP, width)
    returned = lax.all_to_all(results, "expert", split_axis=0, concat_axis=0, tiled=True)
    fetched = jnp.take(returned.reshape(experts * CAP, width), slot_of, axis=0).reshape(
        tok_rows, TOPK, width
    )
    scales = jnp.where(slot_kept, gate_weights.reshape(-1), jnp.float32(0.0)).reshape(
        tok_rows, TOPK, 1
    )
    moe_output = jnp.sum(scales * fetched, axis=1).astype(jnp.bfloat16)
    expert_peak = lax.pmax(local_peak, "replica")
    return (moe_output, moved_gate, moved_up, moved_down, expert_peak.reshape(1))


def solution(mesh):
    placed = (
        P(("expert", "replica"), None),
        P(("expert", "replica"), None),
        P(("expert", "replica"), None),
        P(),
        P(),
        P(),
        P("expert", "replica", None),
        P("expert", "replica", None),
        P("expert", "replica", None),
    )
    return jax.shard_map(
        shards,
        mesh=mesh,
        in_specs=placed,
        out_specs=(
            P(("expert", "replica"), None),
            P("expert", "replica", None),
            P("expert", "replica", None),
            P("expert", "replica", None),
            P("expert"),
        ),
        check_vma=False,
    )
```

profile of v0, /device:TPU:2, one launch (start us, length us, event | category | flops | bytes accessed | tf_op | source)
XLA Modules:
  0.0 886.4 jit_solution(17751766660079716728)
XLA Ops:
  13.0 11.4 %reduce.13 = bf16[32,24576]{1,0:T(8,128)(2,1)} reduce(bf16[32,1,24576]{2,1,0:T(2,128)(2,1)S(1)} %all_to_all.65, bf16[]{:T(256)} %broadcast.166), dimensions={1}, to_apply=%all_to_all.65.reduce_sub_computation | reduce | bytes 3145730 | tf_op jit(solution)/shard_map/all_to_all | solution.py:63
  27.6 9.5 %all-to-all-start.1 = ((bf16[32,2,12288]{2,1,0:T(2,128)(2,1)}), bf16[32,2,12288]{2,1,0:T(2,128)(2,1)}, u32[]{:S(2)}, u32[]{:S(2)}) async-start(bf16[32,2,12288]{2,1,0:T(2,128)(2,1)} %reshape.259), calls=%async_computation.1 | async-start | bytes 3145728 | tf_op jit(solution)/shard_map/all_to_all | solution.py:63
  42.5 11.4 %reduce.12 = bf16[32,24576]{1,0:T(8,128)(2,1)} reduce(bf16[32,1,24576]{2,1,0:T(2,128)(2,1)S(1)} %all_to_all.66, bf16[]{:T(256)} %broadcast.166), dimensions={1}, to_apply=%all_to_all.66.reduce_sub_computation | reduce | bytes 3145730 | tf_op jit(solution)/shard_map/all_to_all | solution.py:66
  57.1 17.1 %all-to-all-done.1 = bf16[32,2,12288]{2,1,0:T(2,128)(2,1)} async-done(((bf16[32,2,12288]{2,1,0:T(2,128)(2,1)}), bf16[32,2,12288]{2,1,0:T(2,128)(2,1)}, u32[]{:S(2)}, u32[]{:S(2)}) %all-to-all-start.1) | async-done | bytes 1572896 | tf_op jit(solution)/shard_map/all_to_all | solution.py:63
  86.1 11.4 %reduce.11 = bf16[32,24576]{1,0:T(8,128)(2,1)} reduce(bf16[32,1,24576]{2,1,0:T(2,128)(2,1)S(1)} %all_to_all.67, bf16[]{:T(256)} %broadcast.166), dimensions={1}, to_apply=%all_to_all.67.reduce_sub_computation | reduce | bytes 3145730 | tf_op jit(solution)/shard_map/all_to_all | solution.py:69
  100.7 17.1 %all-to-all-done.3 = bf16[32,2,12288]{2,1,0:T(2,128)(2,1)} async-done(((bf16[32,2,12288]{2,1,0:T(2,128)(2,1)}), bf16[32,2,12288]{2,1,0:T(2,128)(2,1)}, u32[]{:S(2)}, u32[]{:S(2)}) %all-to-all-start.3) | async-done | bytes 1572896 | tf_op jit(solution)/shard_map/all_to_all | solution.py:66
  124.2 9.5 %reshape.260 = bf16[32,1,24576]{2,1,0:T(2,128)(2,1)} reshape(bf16[32,2,12288]{2,1,0:T(2,128)(2,1)} %all-to-all-done.1) | data formatting | bytes 3145728
  137.3 9.5 %reshape.256 = bf16[32,1,24576]{2,1,0:T(2,128)(2,1)} reshape(bf16[32,2,12288]{2,1,0:T(2,128)(2,1)} %all-to-all-done.3) | data formatting | bytes 3145728
  161.1 9.5 %reshape.264 = bf16[32,1,24576]{2,1,0:T(2,128)(2,1)} reshape(bf16[32,2,12288]{2,1,0:T(2,128)(2,1)} %all-to-all-done.5) | data formatting | bytes 3145728
  199.8 31.5 %all-to-all-done.2 = bf16[32,2,12288]{2,1,0:T(2,128)(2,1)} async-done(((bf16[32,2,12288]{2,1,0:T(2,128)(2,1)}), bf16[32,2,12288]{2,1,0:T(2,128)(2,1)}, u32[]{:S(2)}, u32[]{:S(2)}) %all-to-all-start.2) | async-done | bytes 1572896 | tf_op jit(solution)/shard_map/all_to_all | solution.py:75
  237.2 67.2 %all_gather.6 = s32[64,8]{1,0:T(8,128)S(1)} all-gather(s32[8,8]{1,0:T(8,128)S(1)} %copy-done.5), channel_id=1, replica_groups=mesh['expert'=32,'replica'=8] {'replica'}, dimensions={0}, use_global_device_ids=true | all-gather | bytes 2304 | tf_op jit(solution)/shard_map/all_gather | solution.py:85
  322.6 60.6 %all_gather.7 = bf16[64,4096]{1,0:T(8,128)(2,1)S(1)} all-gather(bf16[8,4096]{1,0:T(8,128)(2,1)S(1)} %copy-done.4), channel_id=1, replica_groups=mesh['expert'=32,'replica'=8] {'replica'}, dimensions={0}, use_global_device_ids=true | all-gather | bytes 589824 | tf_op jit(solution)/shard_map/all_gather | solution.py:84
  391.0 13.1 %gather.16 = bf16[8,32,4,4096]{3,2,1,0:T(4,128)(2,1)} reshape(bf16[1024,4096]{1,0:T(8,128)(2,1)} %gather_fusion) | data formatting | bytes 16777216 | tf_op jit(solution)/shard_map/jit(_take)/gather | solution.py:92
  405.0 8.6 fusion
  422.0 9.9 %reshape.262 = bf16[32,1,24576]{2,1,0:T(2,128)(2,1)} reshape(bf16[32,2,12288]{2,1,0:T(2,128)(2,1)} %all-to-all-done.2) | data formatting | bytes 3145728
  431.9 11.2 %reduce.2 = bf16[32,24576]{1,0:T(8,128)(2,1)S(1)} reduce(bf16[32,1,24576]{2,1,0:T(2,128)(2,1)} %reshape.262, bf16[]{:T(256)} %constant.99), dimensions={1}, to_apply=%all_to_all.53.reduce_sub_computation | reduce | bytes 3145730 | tf_op jit(solution)/shard_map/all_to_all | solution.py:75
  449.9 11.2 %reduce.3 = bf16[32,24576]{1,0:T(8,128)(2,1)S(1)} reduce(bf16[32,1,24576]{2,1,0:T(2,128)(2,1)} %reshape.258, bf16[]{:T(256)} %constant.99), dimensions={1}, to_apply=%all_to_all.58.reduce_sub_computation | reduce | bytes 3145730 | tf_op jit(solution)/shard_map/all_to_all | solution.py:76
  463.8 9.7 %reshape.266 = bf16[32,1,24576]{2,1,0:T(2,128)(2,1)} reshape(bf16[32,2,12288]{2,1,0:T(2,128)(2,1)} %all-to-all-done.6) | data formatting | bytes 3145728
  473.5 12.3 %reduce.4 = bf16[32,24576]{1,0:T(8,128)(2,1)} reduce(bf16[32,1,24576]{2,1,0:T(2,128)(2,1)} %reshape.266, bf16[]{:T(256)} %constant.99), dimensions={1}, to_apply=%all_to_all.63.reduce_sub_computation | reduce | bytes 3145730 | tf_op jit(solution)/shard_map/all_to_all | solution.py:77
  489.6 115.8 %all-to-all-done = bf16[8,32,4,4096]{3,2,0,1:T(4,128)(2,1)} async-done(((bf16[8,32,4,4096]{3,2,0,1:T(4,128)(2,1)}), bf16[8,32,4,4096]{3,2,0,1:T(4,128)(2,1)}, u32[]{:S(2)}, u32[]{:S(2)}) %all-to-all-start) | async-done | bytes 8388640 | tf_op jit(solution)/shard_map/all_to_all | solution.py:95
  605.5 8.5 copy.66
  614.0 12.7 %reshape.188 = bf16[1024,4096]{1,0:T(8,128)(2,1)} reshape(bf16[8,32,4,4096]{3,2,1,0:T(4,128)(2,1)} %copy.66) | data formatting | bytes 16777216 | tf_op jit(solution)/shard_map/reshape | solution.py:44
  642.8 184.3 %reduce-scatter.2.cloned.1.call-done = bf16[128,4096]{1,0:T(8,128)(2,1)} async-done(((bf16[1024,4096]{1,0:T(8,128)(2,1)}), bf16[128,4096]{1,0:T(8,128)(2,1)}) %reduce-scatter.2.cloned.1.call-update) | async-done | bytes 1048592 | tf_op jit(solution)/shard_map/reduce_scatter | solution.py:110
  845.1 30.6 %pmax.7 = f32[1]{0:T(128)} all-reduce(bf16[1]{0:T(256)(128)(2,1)} %bitcast.14), channel_id=1, replica_groups=mesh['expert'=32,'replica'=8] {'replica'}, use_global_device_ids=true, to_apply=%region_11.13 | all-reduce | flops 1 | bytes 6 | tf_op jit(solution)/shard_map/pmax | solution.py:125
  (99 shorter events, 177.9 us)
Async XLA Ops:
  27.6 46.5 %all-to-all-start.1 = ((bf16[32,2,12288]{2,1,0:T(2,128)(2,1)}), bf16[32,2,12288]{2,1,0:T(2,128)(2,1)}, u32[]{:S(2)}, u32[]{:S(2)}) async-start(bf16[32,2,12288]{2,1,0:T(2,128)(2,1)} %reshape.259), calls=%async_computation.1 | async-start | bytes 3145728 | tf_op jit(solution)/shard_map/all_to_all | solution.py:63
  74.2 43.6 %all-to-all-start.3 = ((bf16[32,2,12288]{2,1,0:T(2,128)(2,1)}), bf16[32,2,12288]{2,1,0:T(2,128)(2,1)}, u32[]{:S(2)}, u32[]{:S(2)}) async-start(bf16[32,2,12288]{2,1,0:T(2,128)(2,1)} %reshape.255), calls=%async_computation.3 | async-start | bytes 3145728 | tf_op jit(solution)/shard_map/all_to_all | solution.py:66
  100.7 23.4 %copy-start.7 = (s32[8,2]{0,1:T(2,128)S(1)}, s32[8,2]{0,1:T(2,128)}, u32[]{:S(2)}) copy-start(s32[8,2]{0,1:T(2,128)} %param.15) | copy-start | bytes 196
  117.7 43.3 %all-to-all-start.5 = ((bf16[32,2,12288]{2,1,0:T(2,128)(2,1)}), bf16[32,2,12288]{2,1,0:T(2,128)(2,1)}, u32[]{:S(2)}, u32[]{:S(2)}) async-start(bf16[32,2,12288]{2,1,0:T(2,128)(2,1)} %reshape.263), calls=%async_computation.5 | async-start | bytes 3145728 | tf_op jit(solution)/shard_map/all_to_all | solution.py:69
  188.1 43.2 %all-to-all-start.2 = ((bf16[32,2,12288]{2,1,0:T(2,128)(2,1)}), bf16[32,2,12288]{2,1,0:T(2,128)(2,1)}, u32[]{:S(2)}, u32[]{:S(2)}) async-start(bf16[32,2,12288]{2,1,0:T(2,128)(2,1)} %reshape.261), calls=%async_computation.2 | async-start | bytes 3145728 | tf_op jit(solution)/shard_map/all_to_all | solution.py:75
  199.8 37.4 %copy-start.5 = (s32[8,8]{1,0:T(8,128)S(1)}, s32[8,8]{1,0:T(8,128)}, u32[]{:S(2)}) copy-start(s32[8,8]{1,0:T(8,128)} %param.12) | copy-start | bytes 772
  199.8 104.9 %copy-start.9 = (s32[32]{0:T(128)S(1)}, s32[32]{0:T(128)}, u32[]{:S(2)}) copy-start(s32[32]{0:T(128)} %param.14) | copy-start | bytes 388
  231.3 80.6 %all-to-all-start.4 = ((bf16[32,2,12288]{2,1,0:T(2,128)(2,1)}), bf16[32,2,12288]{2,1,0:T(2,128)(2,1)S(1)}, u32[]{:S(2)}, u32[]{:S(2)}) async-start(bf16[32,2,12288]{2,1,0:T(2,128)(2,1)} %reshape.257), calls=%async_computation.4 | async-start | bytes 3145728 | tf_op jit(solution)/shard_map/all_to_all | solution.py:76
  311.9 7.9 copy-start.8
  311.9 10.7 %copy-start.4 = (bf16[8,4096]{1,0:T(8,128)(2,1)S(1)}, bf16[8,4096]{1,0:T(8,128)(2,1)}, u32[]{:S(2)}) copy-start(bf16[8,4096]{1,0:T(8,128)(2,1)} %param.11) | copy-start | bytes 196612
  311.9 101.7 %all-to-all-start.6 = ((bf16[32,2,12288]{2,1,0:T(2,128)(2,1)}), bf16[32,2,12288]{2,1,0:T(2,128)(2,1)}, u32[]{:S(2)}, u32[]{:S(2)}) async-start(bf16[32,2,12288]{2,1,0:T(2,128)(2,1)} %reshape.265), calls=%async_computation.6 | async-start | bytes 3145728 | tf_op jit(solution)/shard_map/all_to_all | solution.py:77
  413.6 191.8 %all-to-all-start = ((bf16[8,32,4,4096]{3,2,0,1:T(4,128)(2,1)}), bf16[8,32,4,4096]{3,2,0,1:T(4,128)(2,1)}, u32[]{:S(2)}, u32[]{:S(2)}) async-start(bf16[8,32,4,4096]{3,2,0,1:T(4,128)(2,1)} %fusion), calls=%async_computation | async-start | bytes 16777216 | tf_op jit(solution)/shard_map/all_to_all | solution.py:95
  421.9 405.2 %reduce-scatter.2.cloned.1.call-start = ((), (), s32[]{:S(2)}) async-start(), calls=%async_computation.9 | async-start | bytes 9437184 | tf_op jit(solution)/shard_map/reduce_scatter | solution.py:110
  626.7 6.9 copy-start.1
  626.7 6.9 copy-start.3
  633.6 3.6 copy-start.2
  829.4 7.6 copy-start.6
  829.4 46.4 %all-to-all-start.7 = ((bf16[32,4,4096]{2,1,0:T(4,128)(2,1)}), bf16[32,4,4096]{2,1,0:T(4,128)(2,1)}, u32[]{:S(2)}, u32[]{:S(2)}) async-start(bf16[32,4,4096]{2,1,0:T(4,128)(2,1)} %reshape.189), calls=%async_computation.8 | async-start | bytes 2097152 | tf_op jit(solution)/shard_map/all_to_all | solution.py:117
  839.7 2.7 copy-start
Sparse Core Ops, SparseCore 0:
  643.0 184.1 reduce-scatter.1
where the time goes:
time: 898 us; the launch traced here: 886 us
  waiting for transfers between devices  371 us (41%)
  local copies, waits for them, and re-layouts  172 us (19%)
  blocking collectives  159 us (18%)
  other arithmetic  96.1 us (11%)
  starting transfers between devices  57.5 us (6%)
  matrix products  16 us (2%)
  between operations  14.8 us (2%)
    reduce_scatter x1, waiting for transfers between devices, shards(): lax.psum_scatter(jnp.dot(hidden_rows, down_local, preferred_element_type=...  184 us
    all_to_all x1, waiting for transfers between devices, shards(): lax.all_to_all(outgoing.reshape(replicas, experts, CAP, width), 'expert',...  116 us
    unnamed x35, local copies, waits for them, and re-layouts  82.2 us
    all_gather x1, blocking collectives, shards(): lax.all_gather(expert_ids, 'replica', axis=0, tiled=True)  67.2 us
    all_gather x1, blocking collectives, shards(): lax.all_gather(tokens, 'replica', axis=0, tiled=True)  60.6 us
    all_to_all x1, waiting for transfers between devices, shards(): lax.all_to_all(arranged[0], 'expert', split_axis=0, concat_axis=0, tiled=...  31.5 us
    pmax x1, blocking collectives, shards(): expert_peak = lax.pmax(local_peak, 'replica')  30.6 us
    gather x2, local copies, waits for them, and re-layouts, shards(): picked = jnp.take(group_tokens, source_all + starts, axis=0)  20.9 us
  transfers between devices with their start and end apart: 9, of which 6 were waited for; matrix products, arithmetic and copies ran while one was open for 21% of the time, Pallas kernels for 0%

commit v1 on v0

--- a/solution.py
+++ b/solution.py
@@ -82,7 +82,10 @@
     gate_local, up_local, down_local = (moved_gate[0], moved_up[0], moved_down[0])
     group_tokens, group_ids = (
         lax.all_gather(tokens, "replica", axis=0, tiled=True),
-        lax.all_gather(expert_ids, "replica", axis=0, tiled=True),
+        jnp.concatenate(
+            lax.all_to_all(jnp.stack([expert_ids] * lax.axis_size("replica")), "replica", 0, 0),
+            axis=0,
+        ),
     )
     group_ids = group_ids.reshape(replicas, tok_rows, TOPK)
     slot_all, kept_all, source_all, filled_all = jax.vmap(route_slots, in_axes=(0, None, None))(

time: 898 us -> 874 us (0.973)
  blocking collectives: 159 us -> 102 us
  waiting for transfers between devices: 371 us -> 396 us
    all_gather x1 -> x0, blocking collectives: 67.2 us -> none  [shards(): lax.all_gather(expert_ids, 'replica', axis=0, tiled=True)]
    all_to_all x1, waiting for transfers between devices: 0.01 us -> 31.2 us  [shards(): lax.all_to_all(arranged[1], 'expert', split_axis=0, concat_axis=0, tiled=...]
    all_gather x1, blocking collectives: 60.6 us -> 71.2 us  [shards(): lax.all_gather(tokens, 'replica', axis=0, tiled=True)]
  transfers between devices with their start and end apart: 9 -> 10, of which waited for: 6 -> 7; matrix products, arithmetic and copies ran while one was open for 21% -> 24% of each run, Pallas kernels for 0% -> 0%
where the time goes in v1:
time: 874 us; the launch traced here: 862 us
  waiting for transfers between devices  396 us (45%)
  local copies, waits for them, and re-layouts  172 us (20%)
  blocking collectives  102 us (12%)
  other arithmetic  96.1 us (11%)
  starting transfers between devices  64.5 us (7%)
  matrix products  16 us (2%)
  between operations  14.8 us (2%)
    reduce_scatter x1, waiting for transfers between devices, shards(): lax.psum_scatter(jnp.dot(hidden_rows, down_local, preferred_element_type=...  178 us
    all_to_all x1, waiting for transfers between devices, shards(): lax.all_to_all(outgoing.reshape(replicas, experts, CAP, width), 'expert',...  116 us
    unnamed x35, local copies, waits for them, and re-layouts  81.6 us
    all_gather x1, blocking collectives, shards(): lax.all_gather(tokens, 'replica', axis=0, tiled=True)  71.2 us
    all_to_all x1, waiting for transfers between devices, shards(): lax.all_to_all(arranged[0], 'expert', split_axis=0, concat_axis=0, tiled=...  31.5 us
    all_to_all x1, waiting for transfers between devices, shards(): lax.all_to_all(arranged[1], 'expert', split_axis=0, concat_axis=0, tiled=...  31.2 us
    pmax x1, blocking collectives, shards(): expert_peak = lax.pmax(local_peak, 'replica')  30.6 us
    gather x2, local copies, waits for them, and re-layouts, shards(): picked = jnp.take(group_tokens, source_all + starts, axis=0)  20.9 us
  transfers between devices with their start and end apart: 10, of which 7 were waited for; matrix products, arithmetic and copies ran while one was open for 24% of the time, Pallas kernels for 0%

profile of v1, /device:TPU:2, one launch (start us, length us, event | category | flops | bytes accessed | tf_op | source)
XLA Modules:
  0.0 861.9 jit_solution(7012255662546275042)
XLA Ops:
  13.0 11.4 %reduce.13 = bf16[32,24576]{1,0:T(8,128)(2,1)} reduce(bf16[32,1,24576]{2,1,0:T(2,128)(2,1)S(1)} %all_to_all.69, bf16[]{:T(256)} %broadcast.168), dimensions={1}, to_apply=%all_to_all.69.reduce_sub_computation | reduce | bytes 3145730 | tf_op jit(solution)/shard_map/all_to_all | solution.py:63
  27.6 9.5 %all-to-all-start.2 = ((bf16[32,2,12288]{2,1,0:T(2,128)(2,1)}), bf16[32,2,12288]{2,1,0:T(2,128)(2,1)}, u32[]{:S(2)}, u32[]{:S(2)}) async-start(bf16[32,2,12288]{2,1,0:T(2,128)(2,1)} %reshape.261), calls=%async_computation.2 | async-start | bytes 3145728 | tf_op jit(solution)/shard_map/all_to_all | solution.py:63
  42.5 11.4 %reduce.12 = bf16[32,24576]{1,0:T(8,128)(2,1)} reduce(bf16[32,1,24576]{2,1,0:T(2,128)(2,1)S(1)} %all_to_all.70, bf16[]{:T(256)} %broadcast.168), dimensions={1}, to_apply=%all_to_all.70.reduce_sub_computation | reduce | bytes 3145730 | tf_op jit(solution)/shard_map/all_to_all | solution.py:66
  57.1 17.1 %all-to-all-done.2 = bf16[32,2,12288]{2,1,0:T(2,128)(2,1)} async-done(((bf16[32,2,12288]{2,1,0:T(2,128)(2,1)}), bf16[32,2,12288]{2,1,0:T(2,128)(2,1)}, u32[]{:S(2)}, u32[]{:S(2)}) %all-to-all-start.2) | async-done | bytes 1572896 | tf_op jit(solution)/shard_map/all_to_all | solution.py:63
  86.1 11.4 %reduce.11 = bf16[32,24576]{1,0:T(8,128)(2,1)} reduce(bf16[32,1,24576]{2,1,0:T(2,128)(2,1)S(1)} %all_to_all.71, bf16[]{:T(256)} %broadcast.168), dimensions={1}, to_apply=%all_to_all.71.reduce_sub_computation | reduce | bytes 3145730 | tf_op jit(solution)/shard_map/all_to_all | solution.py:69
  100.7 17.1 %all-to-all-done.4 = bf16[32,2,12288]{2,1,0:T(2,128)(2,1)} async-done(((bf16[32,2,12288]{2,1,0:T(2,128)(2,1)}), bf16[32,2,12288]{2,1,0:T(2,128)(2,1)}, u32[]{:S(2)}, u32[]{:S(2)}) %all-to-all-start.4) | async-done | bytes 1572896 | tf_op jit(solution)/shard_map/all_to_all | solution.py:66
  124.2 9.5 %reshape.262 = bf16[32,1,24576]{2,1,0:T(2,128)(2,1)} reshape(bf16[32,2,12288]{2,1,0:T(2,128)(2,1)} %all-to-all-done.2) | data formatting | bytes 3145728
  137.3 9.5 %reshape.258 = bf16[32,1,24576]{2,1,0:T(2,128)(2,1)} reshape(bf16[32,2,12288]{2,1,0:T(2,128)(2,1)} %all-to-all-done.4) | data formatting | bytes 3145728
  161.7 8.6 %all-to-all-start = ((s32[8,8,8]{2,1,0:T(8,128)}), s32[8,8,8]{2,1,0:T(8,128)S(1)}, u32[]{:S(2)}, u32[]{:S(2)}) async-start(s32[8,8,8]{2,1,0:T(8,128)} %stack.2), calls=%async_computation | async-start | bytes 65536 | tf_op jit(solution)/shard_map/all_to_all | solution.py:86
  170.3 9.5 %reshape.266 = bf16[32,1,24576]{2,1,0:T(2,128)(2,1)} reshape(bf16[32,2,12288]{2,1,0:T(2,128)(2,1)} %all-to-all-done.6) | data formatting | bytes 3145728
  208.9 31.5 %all-to-all-done.3 = bf16[32,2,12288]{2,1,0:T(2,128)(2,1)} async-done(((bf16[32,2,12288]{2,1,0:T(2,128)(2,1)}), bf16[32,2,12288]{2,1,0:T(2,128)(2,1)}, u32[]{:S(2)}, u32[]{:S(2)}) %all-to-all-start.3) | async-done | bytes 1572896 | tf_op jit(solution)/shard_map/all_to_all | solution.py:75
  252.2 31.2 %all-to-all-done.5 = bf16[32,2,12288]{2,1,0:T(2,128)(2,1)S(1)} async-done(((bf16[32,2,12288]{2,1,0:T(2,128)(2,1)}), bf16[32,2,12288]{2,1,0:T(2,128)(2,1)S(1)}, u32[]{:S(2)}, u32[]{:S(2)}) %all-to-all-start.5) | async-done | bytes 1572896 | tf_op jit(solution)/shard_map/all_to_all | solution.py:76
  289.4 71.2 %all_gather.3 = bf16[64,4096]{1,0:T(8,128)(2,1)S(1)} all-gather(bf16[8,4096]{1,0:T(8,128)(2,1)S(1)} %copy-done.4), channel_id=1, replica_groups=mesh['expert'=32,'replica'=8] {'replica'}, dimensions={0}, use_global_device_ids=true | all-gather | bytes 589824 | tf_op jit(solution)/shard_map/all_gather | solution.py:84
  372.7 13.1 %gather.16 = bf16[8,32,4,4096]{3,2,1,0:T(4,128)(2,1)} reshape(bf16[1024,4096]{1,0:T(8,128)(2,1)} %gather_fusion) | data formatting | bytes 16777216 | tf_op jit(solution)/shard_map/jit(_take)/gather | solution.py:95
  386.7 8.6 fusion
  404.0 9.5 %reshape.264 = bf16[32,1,24576]{2,1,0:T(2,128)(2,1)} reshape(bf16[32,2,12288]{2,1,0:T(2,128)(2,1)} %all-to-all-done.3) | data formatting | bytes 3145728
  413.5 11.2 %reduce.2 = bf16[32,24576]{1,0:T(8,128)(2,1)S(1)} reduce(bf16[32,1,24576]{2,1,0:T(2,128)(2,1)} %reshape.264, bf16[]{:T(256)} %constant.99), dimensions={1}, to_apply=%all_to_all.57.reduce_sub_computation | reduce | bytes 3145730 | tf_op jit(solution)/shard_map/all_to_all | solution.py:75
  431.5 11.2 %reduce.3 = bf16[32,24576]{1,0:T(8,128)(2,1)S(1)} reduce(bf16[32,1,24576]{2,1,0:T(2,128)(2,1)} %reshape.260, bf16[]{:T(256)} %constant.99), dimensions={1}, to_apply=%all_to_all.62.reduce_sub_computation | reduce | bytes 3145730 | tf_op jit(solution)/shard_map/all_to_all | solution.py:76
  445.4 9.7 %reshape.268 = bf16[32,1,24576]{2,1,0:T(2,128)(2,1)} reshape(bf16[32,2,12288]{2,1,0:T(2,128)(2,1)} %all-to-all-done.7) | data formatting | bytes 3145728
  455.1 12.3 %reduce.4 = bf16[32,24576]{1,0:T(8,128)(2,1)} reduce(bf16[32,1,24576]{2,1,0:T(2,128)(2,1)} %reshape.268, bf16[]{:T(256)} %constant.99), dimensions={1}, to_apply=%all_to_all.67.reduce_sub_computation | reduce | bytes 3145730 | tf_op jit(solution)/shard_map/all_to_all | solution.py:77
  471.2 115.8 %all-to-all-done.1 = bf16[8,32,4,4096]{3,2,0,1:T(4,128)(2,1)} async-done(((bf16[8,32,4,4096]{3,2,0,1:T(4,128)(2,1)}), bf16[8,32,4,4096]{3,2,0,1:T(4,128)(2,1)}, u32[]{:S(2)}, u32[]{:S(2)}) %all-to-all-start.1) | async-done | bytes 8388640 | tf_op jit(solution)/shard_map/all_to_all | solution.py:98
  595.5 12.7 %reshape.190 = bf16[1024,4096]{1,0:T(8,128)(2,1)} reshape(bf16[8,32,4,4096]{3,2,1,0:T(4,128)(2,1)} %copy.63) | data formatting | bytes 16777216 | tf_op jit(solution)/shard_map/reshape | solution.py:44
  624.4 178.3 %reduce-scatter.2.cloned.1.call-done = bf16[128,4096]{1,0:T(8,128)(2,1)} async-done(((bf16[1024,4096]{1,0:T(8,128)(2,1)}), bf16[128,4096]{1,0:T(8,128)(2,1)}) %reduce-scatter.2.cloned.1.call-update) | async-done | bytes 1048592 | tf_op jit(solution)/shard_map/reduce_scatter | solution.py:113
  820.7 30.6 %pmax.7 = f32[1]{0:T(128)} all-reduce(bf16[1]{0:T(256)(128)(2,1)} %bitcast.15), channel_id=1, replica_groups=mesh['expert'=32,'replica'=8] {'replica'}, use_global_device_ids=true, to_apply=%region_11.13 | all-reduce | flops 1 | bytes 6 | tf_op jit(solution)/shard_map/pmax | solution.py:128
  (100 shorter events, 185.2 us)
Async XLA Ops:
  27.6 46.5 %all-to-all-start.2 = ((bf16[32,2,12288]{2,1,0:T(2,128)(2,1)}), bf16[32,2,12288]{2,1,0:T(2,128)(2,1)}, u32[]{:S(2)}, u32[]{:S(2)}) async-start(bf16[32,2,12288]{2,1,0:T(2,128)(2,1)} %reshape.261), calls=%async_computation.2 | async-start | bytes 3145728 | tf_op jit(solution)/shard_map/all_to_all | solution.py:63
  74.2 43.6 %all-to-all-start.4 = ((bf16[32,2,12288]{2,1,0:T(2,128)(2,1)}), bf16[32,2,12288]{2,1,0:T(2,128)(2,1)}, u32[]{:S(2)}, u32[]{:S(2)}) async-start(bf16[32,2,12288]{2,1,0:T(2,128)(2,1)} %reshape.257), calls=%async_computation.4 | async-start | bytes 3145728 | tf_op jit(solution)/shard_map/all_to_all | solution.py:66
  100.7 23.4 %copy-start.7 = (s32[8,2]{0,1:T(2,128)S(1)}, s32[8,2]{0,1:T(2,128)}, u32[]{:S(2)}) copy-start(s32[8,2]{0,1:T(2,128)} %param.15) | copy-start | bytes 196
  117.7 43.3 %all-to-all-start.6 = ((bf16[32,2,12288]{2,1,0:T(2,128)(2,1)}), bf16[32,2,12288]{2,1,0:T(2,128)(2,1)}, u32[]{:S(2)}, u32[]{:S(2)}) async-start(bf16[32,2,12288]{2,1,0:T(2,128)(2,1)} %reshape.265), calls=%async_computation.6 | async-start | bytes 3145728 | tf_op jit(solution)/shard_map/all_to_all | solution.py:69
  153.1 7.9 copy-start.5
  161.7 35.5 %all-to-all-start = ((s32[8,8,8]{2,1,0:T(8,128)}), s32[8,8,8]{2,1,0:T(8,128)S(1)}, u32[]{:S(2)}, u32[]{:S(2)}) async-start(s32[8,8,8]{2,1,0:T(8,128)} %stack.2), calls=%async_computation | async-start | bytes 65536 | tf_op jit(solution)/shard_map/all_to_all | solution.py:86
  197.2 43.2 %all-to-all-start.3 = ((bf16[32,2,12288]{2,1,0:T(2,128)(2,1)}), bf16[32,2,12288]{2,1,0:T(2,128)(2,1)}, u32[]{:S(2)}, u32[]{:S(2)}) async-start(bf16[32,2,12288]{2,1,0:T(2,128)(2,1)} %reshape.263), calls=%async_computation.3 | async-start | bytes 3145728 | tf_op jit(solution)/shard_map/all_to_all | solution.py:75
  208.9 37.5 %copy-start.9 = (s32[32]{0:T(128)S(1)}, s32[32]{0:T(128)}, u32[]{:S(2)}) copy-start(s32[32]{0:T(128)} %param.14) | copy-start | bytes 388
  240.4 43.1 %all-to-all-start.5 = ((bf16[32,2,12288]{2,1,0:T(2,128)(2,1)}), bf16[32,2,12288]{2,1,0:T(2,128)(2,1)S(1)}, u32[]{:S(2)}, u32[]{:S(2)}) async-start(bf16[32,2,12288]{2,1,0:T(2,128)(2,1)} %reshape.259), calls=%async_computation.5 | async-start | bytes 3145728 | tf_op jit(solution)/shard_map/all_to_all | solution.py:76
  252.2 37.2 %copy-start.4 = (bf16[8,4096]{1,0:T(8,128)(2,1)S(1)}, bf16[8,4096]{1,0:T(8,128)(2,1)}, u32[]{:S(2)}) copy-start(bf16[8,4096]{1,0:T(8,128)(2,1)} %param.11) | copy-start | bytes 196612
  252.2 108.5 %copy-start.8 = (s32[32]{0:T(128)S(1)}, s32[32]{0:T(128)}, u32[]{:S(2)}) copy-start(s32[32]{0:T(128)} %param.16) | copy-start | bytes 388
  283.4 111.8 %all-to-all-start.7 = ((bf16[32,2,12288]{2,1,0:T(2,128)(2,1)}), bf16[32,2,12288]{2,1,0:T(2,128)(2,1)}, u32[]{:S(2)}, u32[]{:S(2)}) async-start(bf16[32,2,12288]{2,1,0:T(2,128)(2,1)} %reshape.267), calls=%async_computation.7 | async-start | bytes 3145728 | tf_op jit(solution)/shard_map/all_to_all | solution.py:77
  395.2 191.8 %all-to-all-start.1 = ((bf16[8,32,4,4096]{3,2,0,1:T(4,128)(2,1)}), bf16[8,32,4,4096]{3,2,0,1:T(4,128)(2,1)}, u32[]{:S(2)}, u32[]{:S(2)}) async-start(bf16[8,32,4,4096]{3,2,0,1:T(4,128)(2,1)} %fusion), calls=%async_computation.1 | async-start | bytes 16777216 | tf_op jit(solution)/shard_map/all_to_all | solution.py:98
  403.5 399.2 %reduce-scatter.2.cloned.1.call-start = ((), (), s32[]{:S(2)}) async-start(), calls=%async_computation.10 | async-start | bytes 9437184 | tf_op jit(solution)/shard_map/reduce_scatter | solution.py:113
  608.3 6.9 copy-start.1
  608.3 6.9 copy-start.3
  615.2 3.6 copy-start.2
  805.0 7.5 copy-start.6
  805.0 46.4 %all-to-all-start.8 = ((bf16[32,4,4096]{2,1,0:T(4,128)(2,1)}), bf16[32,4,4096]{2,1,0:T(4,128)(2,1)}, u32[]{:S(2)}, u32[]{:S(2)}) async-start(bf16[32,4,4096]{2,1,0:T(4,128)(2,1)} %reshape.191), calls=%async_computation.9 | async-start | bytes 2097152 | tf_op jit(solution)/shard_map/all_to_all | solution.py:120
  815.3 2.7 copy-start
Sparse Core Ops, SparseCore 0:
  624.5 178.1 reduce-scatter.1
